TPU v7x, 256 devices: a whole 4x4x8 slice. The times are simulated.
256 devices in a mesh: ctx: 4 (over x_hi, core), exp: 64 (over y, z, x_lo).
Axes of the slice: x: 4 (x_hi: 2, x_lo: 2; x = x_hi * 2 + x_lo), y: 4, z: 8, core: 2. Of those that a mesh axis runs over, the one named last changes fastest.
Arguments:
- queries: bfloat16 [64, 1024, 2048], P('exp', 'ctx'), may hold values from -5 to 5
- key_rows: bfloat16 [64, 1024, 2048], P('exp', 'ctx'), may hold values from -5 to 5
- value_rows: bfloat16 [64, 1024, 2048], P('exp', 'ctx'), may hold values from -6 to 6
- residual_in: bfloat16 [64, 1024, 2048], P('exp', 'ctx'), may hold values from -6 to 6
- norm_gain: float32 [2048], replicated, may hold values from 0.1 to 1.9
- routes: int32 [64, 1024, 2], P('exp', 'ctx'), may hold values from 0 to 63, all different within a row; in each aligned block of 256 rows (0 to 255, 256 to 511, ..., all dimensions but the last counted through in order) at most 10 rows name the same one
- gate_weights: float32 [64, 1024, 2], P('exp', 'ctx'), may hold values from 0.25 to 1
- gate_up_weight: bfloat16 [64, 2048, 2, 1024], P('exp', None, None, 'ctx'), may hold values from -0.125 to 0.125
- down_weight: bfloat16 [64, 1024, 2048], P('exp', 'ctx'), may hold values from -0.1875 to 0.1875
Outputs:
- layer_out: bfloat16 [64, 1024, 2048], P('exp', 'ctx')
Inputs may be any that keep to these rules, and one draw needn't show every extreme that they name: `routes`: within the rows of one device (aligned blocks of 256 tokens in clip-then-frame order), no expert is named more than 10 times; the 2 experts of a token differ.
All inputs are finite; a program needn't handle non-finite values.
Results may differ from a plain program's by a relative error of at most 0.011.
Values may be sent and summed in bfloat16 or wider, within the bound.
No kernel may reach another device: no remote copies, remote signals or barrier semaphores. Data moves between devices by JAX's collectives and lax.ppermute only.
A program may use at most 128 MiB of HBM per device.

v0:
```python
import jax
import jax.numpy as jnp
from jax import lax
from jax.sharding import PartitionSpec as P

HEADS = 16


def shards(
    queries,
    key_rows,
    value_rows,
    residual_in,
    norm_gain,
    routes,
    gate_weights,
    gate_up_weight,
    down_weight,
):
    clip_count, row_count, feature_count = queries.shape
    head_count = HEADS
    head_size = feature_count // head_count
    score_scale = head_size ** (-0.5)
    query_heads = queries.reshape(clip_count, row_count, head_count, head_size)
    running_max = jnp.full((clip_count, row_count, head_count), -1e30, jnp.float32)
    key_part = lax.all_gather(key_rows, "ctx", axis=1, tiled=True)
    value_part = lax.all_gather(value_rows, "ctx", axis=1, tiled=True)
    key_heads = key_part.reshape(clip_count, -1, head_count, head_size)
    value_heads = value_part.reshape(clip_count, -1, head_count, head_size)
    scores = (
        jnp.einsum("cqhd,ckhd->cqhk", query_heads, key_heads, preferred_element_type=jnp.float32)
        * score_scale
    )
    new_max = jnp.maximum(running_max, jnp.max(scores, axis=-1))
    expo = jnp.exp(scores - new_max[..., None])
    running_sum = jnp.sum(expo, axis=-1)
    weighted = jnp.einsum(
        "cqhk,ckhd->cqhd",
        expo.astype(jnp.bfloat16),
        value_heads,
        preferred_element_type=jnp.float32,
    )
    final_max, final_sum, weighted = (new_max, running_sum, weighted)
    attention = (weighted / final_sum[..., None]).reshape(clip_count, row_count, feature_count)
    mixed_rows = (residual_in.astype(jnp.float32) + attention).astype(jnp.bfloat16)
    mixed_float = mixed_rows.astype(jnp.float32)
    mean_square = jnp.mean(mixed_float * mixed_float, axis=-1, keepdims=True)
    normed = (mixed_float * lax.rsqrt(mean_square + 1e-05) * norm_gain).astype(jnp.bfloat16)
    token_count = clip_count * row_count
    top_count = routes.shape[-1]
    expert_count = lax.axis_size("exp") * gate_up_weight.shape[0]
    capacity = max(2, -(-(5 * token_count * top_count) // (4 * expert_count)))
    flat_routes = routes.reshape(-1)
    one_hot = (flat_routes[:, None] == jnp.arange(expert_count, dtype=jnp.int32)[None, :]).astype(
        jnp.int32
    )
    running_count = jnp.cumsum(one_hot, axis=0)
    slot_index = jnp.sum(running_count * one_hot, axis=1) - 1
    destination = flat_routes * capacity + slot_index
    source_rows = jnp.repeat(normed.reshape(token_count, feature_count), top_count, axis=0)
    send_buffer = (
        jnp.zeros((expert_count * capacity, feature_count), jnp.bfloat16)
        .at[destination]
        .set(source_rows)
    )
    send_buffer = send_buffer.reshape(expert_count, capacity, feature_count)
    local_units = down_weight.shape[1]
    portion = lax.all_gather(
        lax.all_to_all(send_buffer, "exp", split_axis=0, concat_axis=0, tiled=True),
        "ctx",
        axis=1,
        tiled=True,
    )
    flattened = portion.reshape(-1, feature_count)
    gate_and_up = jnp.dot(
        flattened,
        gate_up_weight[0].reshape(feature_count, 2 * local_units),
        preferred_element_type=jnp.float32,
    )
    hidden = (jax.nn.silu(gate_and_up[:, :local_units]) * gate_and_up[:, local_units:]).astype(
        jnp.bfloat16
    )
    projected = jnp.dot(hidden, down_weight[0], preferred_element_type=jnp.float32)
    terms = projected.reshape(portion.shape[0], portion.shape[1], feature_count)
    summed = lax.psum_scatter(terms.astype(jnp.bfloat16), "ctx", scatter_dimension=1, tiled=True)
    returned = lax.all_to_all(summed, "exp", split_axis=0, concat_axis=0, tiled=True)
    expert_out = returned.reshape(-1, feature_count)[destination]
    expert_out = expert_out.reshape(token_count, top_count, feature_count).astype(jnp.float32)
    expert_sum = jnp.sum(gate_weights.reshape(token_count, top_count, 1) * expert_out, axis=1)
    layer_out = (mixed_float.reshape(token_count, feature_count) + expert_sum).astype(jnp.bfloat16)
    return layer_out.reshape(clip_count, row_count, feature_count)


def solution(mesh):
    return jax.shard_map(
        shards,
        mesh=mesh,
        in_specs=(
            P("exp", "ctx", None),
            P("exp", "ctx", None),
            P("exp", "ctx", None),
            P("exp", "ctx", None),
            P(),
            P("exp", "ctx", None),
            P("exp", "ctx", None),
            P("exp", None, None, "ctx"),
            P("exp", "ctx", None),
        ),
        out_specs=P("exp", "ctx", None),
        check_vma=False,
    )
```

profile of v0, /device:TPU:4, one launch (start us, length us, event | category | flops | bytes accessed | tf_op | source)
XLA Modules:
  0.0 603.2 jit_solution(17065852235296107918)
XLA Ops:
  12.4 38.6 %all-gather.4.cloned.1.call-done = bf16[1,1024,2048]{1,2,0:T(8,128)(2,1)} async-done(((bf16[1,256,2048]{1,2,0:T(8,128)(2,1)}), bf16[1,1024,2048]{1,2,0:T(8,128)(2,1)}) %all-gather.4.cloned.1.call-update) | async-done | bytes 4194320 | tf_op jit(solution)/shard_map/all_gather | solution.py:26
  51.0 10.3 %bitcast_reduce_fusion = (f32[256,16]{0,1:T(8,128)S(1)}, f32[16,1024,256]{2,1,0:T(8,128)}) fusion(bf16[1024,16,128]{0,2,1:T(8,128)(2,1)} %bitcast.73, bf16[256,16,128]{2,1,0:T(8,128)(2,1)S(1)} %bitcast.71), kind=kOutput, calls=%fused_computation.3 | convolution fusion | flops 1082126336 | bytes 22036480 | tf_op jit(solution)/shard_map/cqhd,ckhd->cqhk/dot_general | solution.py:31
  61.4 8.8 %fusion.1 = f32[256,16]{0,1:T(8,128)S(1)} fusion(f32[16,1024,256]{2,1,0:T(8,128)} %get-tuple-element.8, f32[256,16]{0,1:T(8,128)S(1)} %broadcast_maximum_fusion), kind=kLoop, calls=%fused_computation.5 | loop fusion | flops 12578816 | bytes 16809984 | tf_op jit(solution)/shard_map/reduce_sum | solution.py:36
  70.2 23.2 %all-gather.6.cloned.1.call-done = bf16[1,1024,2048]{2,1,0:T(8,128)(2,1)} async-done(((bf16[1,256,2048]{2,1,0:T(8,128)(2,1)}), bf16[1,1024,2048]{2,1,0:T(8,128)(2,1)}) %all-gather.6.cloned.1.call-update) | async-done | bytes 4194320 | tf_op jit(solution)/shard_map/all_gather | solution.py:27
  93.4 6.4 %copy.58 = bf16[1,1024,2048]{1,2,0:T(8,128)(2,1)} copy(bf16[1,1024,2048]{2,1,0:T(8,128)(2,1)} %all-gather.6.cloned.1.call-done) | data formatting | bytes 8388608 | tf_op jit(solution)/shard_map/all_gather | solution.py:27
  99.8 9.2 %bitcast_divide_fusion = f32[1,256,16,128]{1,3,2,0:T(8,128)S(1)} fusion(bf16[1024,16,128]{0,2,1:T(8,128)(2,1)} %bitcast.72, f32[16,1024,256]{2,1,0:T(8,128)} %get-tuple-element.8, f32[256,16]{0,1:T(8,128)S(1)} %broadcast_maximum_fusion, f32[256,16]{0,1:T(8,128)S(1)} %fusion.1), kind=kOutput, calls=%fused_computation.22 | convolution fusion | flops 1086849024 | bytes 23101440 | tf_op jit(solution)/shard_map/cqhk,ckhd->cqhd/dot_general | solution.py:37
  116.1 4.1 reshape.155
  120.2 6.6 %scatter_custom_fusion = bf16[640,2048]{1,0:T(8,128)(2,1)} fusion(s32[512]{0:T(512)S(1)} %bitcast.78, bf16[512,2048]{1,0:T(8,128)(2,1)} %reshape.155, bf16[]{:T(256)} %constant.8.clone.1), kind=kCustom, calls=%fused_computation.24 | custom fusion | bytes 2621952 | tf_op jit(solution)/shard_map/scatter | solution.py:64
  126.8 5.4 reshape.139
  132.2 109.1 %all_to_all.10 = bf16[64,10,2048]{2,1,0:T(8,128)(2,1)S(1)} all-to-all(bf16[64,10,2048]{2,1,0:T(8,128)(2,1)} %reshape.139), channel_id=1, replica_groups=mesh['ctx'=4,'exp'=64] {'exp'}, dimensions={0} | all-to-all | bytes 5242880 | tf_op jit(solution)/shard_map/all_to_all | solution.py:69
  244.3 3.4 copy.74
  247.7 66.9 %all-gather.8.cloned.1.call-done = bf16[64,40,2048]{2,0,1:T(8,128)(2,1)} async-done(((bf16[64,10,2048]{2,0,1:T(8,128)(2,1)}), bf16[64,40,2048]{2,0,1:T(8,128)(2,1)}) %all-gather.8.cloned.1.call-update) | async-done | bytes 10485776 | tf_op jit(solution)/shard_map/all_gather | solution.py:68
  314.6 13.6 %copy.67 = bf16[64,40,2048]{2,1,0:T(8,128)(2,1)} copy(bf16[64,40,2048]{2,0,1:T(8,128)(2,1)} %all-gather.8.cloned.1.call-done) | data formatting | bytes 20971520 | tf_op jit(solution)/shard_map/all_gather | solution.py:68
  328.2 9.0 %fusion.25 = f32[2560,512]{1,0:T(8,128)S(1)} fusion(bf16[2560,2048]{1,0:T(8,128)(2,1)} %bitcast.69, bf16[2048,512]{1,0:T(8,128)(2,1)} %bitcast.75), kind=kOutput, calls=%fused_computation.45 | convolution fusion | flops 5368709120 | bytes 17825792 | tf_op jit(solution)/shard_map/dot_general | solution.py:75
  338.1 5.8 convolution_convert_fusion
  343.9 13.8 %copy.68 = bf16[64,40,2048]{2,0,1:T(8,128)(2,1)} copy(bf16[64,40,2048]{2,1,0:T(8,128)(2,1)} %convolution_convert_fusion) | data formatting | bytes 20971520 | tf_op jit(solution)/shard_map/convert_element_type | solution.py:85
  357.7 96.1 %reduce-scatter.2.cloned.1.call-done = bf16[64,10,2048]{2,0,1:T(8,128)(2,1)} async-done(((bf16[64,40,2048]{2,0,1:T(8,128)(2,1)}), bf16[64,10,2048]{2,0,1:T(8,128)(2,1)}) %reduce-scatter.2.cloned.1.call-update) | async-done | bytes 2621456 | tf_op jit(solution)/shard_map/reduce_scatter | solution.py:85
  453.8 5.3 copy.69
  459.1 12.8 %all-to-all-start.1 = ((bf16[64,10,2048]{2,1,0:T(8,128)(2,1)}), bf16[64,10,2048]{2,1,0:T(8,128)(2,1)}, u32[]{:S(2)}, u32[]{:S(2)}) async-start(bf16[64,10,2048]{2,1,0:T(8,128)(2,1)} %copy.69), calls=%async_computation.2 | async-start | bytes 8388608 | tf_op jit(solution)/shard_map/all_to_all | solution.py:86
  472.0 95.9 %all-to-all-done.1 = bf16[64,10,2048]{2,1,0:T(8,128)(2,1)} async-done(((bf16[64,10,2048]{2,1,0:T(8,128)(2,1)}), bf16[64,10,2048]{2,1,0:T(8,128)(2,1)}, u32[]{:S(2)}, u32[]{:S(2)}) %all-to-all-start.1) | async-done | bytes 2621472 | tf_op jit(solution)/shard_map/all_to_all | solution.py:86
  567.9 5.5 reshape.141
  573.4 7.4 %gather_fusion = bf16[512,2048]{1,0:T(8,128)(2,1)} fusion(bf16[640,2048]{1,0:T(8,128)(2,1)} %reshape.141, s32[1024]{0:T(1024)S(1)} %pad_clamp_fusion), kind=kCustom, calls=%fused_computation | custom fusion | bytes 4196352 | tf_op jit(solution)/shard_map/gather | solution.py:87
  580.8 5.4 reshape.142
  586.3 8.9 %multiply_reduce_fusion = f32[256,2048]{1,0:T(8,128)S(1)} fusion(f32[256,2,2048]{2,1,0:T(2,128)} %reshape.142, f32[256,2]{1,0:T(8,128)S(1)} %copy.61), kind=kLoop, calls=%fused_computation.12 | loop fusion | flops 1572864 | bytes 6293504 | tf_op jit(solution)/shard_map/reduce_sum | solution.py:89
  (45 shorter events, 18.1 us)
Async XLA Ops:
  6.5 331.6 %copy-start = (bf16[1,256,2048]{2,1,0:T(8,128)(2,1)S(1)}, bf16[1,256,2048]{2,1,0:T(8,128)(2,1)}, u32[]{:S(2)}) copy-start(bf16[1,256,2048]{2,1,0:T(8,128)(2,1)} %param.17) | copy-start | bytes 3145732
  6.5 3.2 copy-start.3
  6.5 3.7 copy-start.1
  6.5 44.5 %all-gather.4.cloned.1.call-start = ((), (), s32[]{:S(2)}) async-start(), calls=%async_computation.3 | async-start | bytes 5242880 | tf_op jit(solution)/shard_map/all_gather | solution.py:26
  9.0 84.4 %all-gather.6.cloned.1.call-start = ((), (), s32[]{:S(2)}) async-start(), calls=%async_computation.4 | async-start | bytes 5242880 | tf_op jit(solution)/shard_map/all_gather | solution.py:27
  9.7 304.9 %all-gather.8.cloned.1.call-start = ((), (), s32[]{:S(2)}) async-start(), calls=%async_computation.5 | async-start | bytes 13107200 | tf_op jit(solution)/shard_map/all_gather | solution.py:68
  110.9 2.3 copy-start.2
  244.3 209.5 %reduce-scatter.2.cloned.1.call-start = ((), (), s32[]{:S(2)}) async-start(), calls=%async_computation.6 | async-start | bytes 13107200 | tf_op jit(solution)/shard_map/reduce_scatter | solution.py:85
  459.1 12.8 %copy-start.4 = (f32[1,256,2]{1,2,0:T(2,128)S(1)}, f32[1,256,2]{1,2,0:T(2,128)}, u32[]{:S(2)}) copy-start(f32[1,256,2]{1,2,0:T(2,128)} %param.15) | copy-start | bytes 6148
  459.1 108.8 %all-to-all-start.1 = ((bf16[64,10,2048]{2,1,0:T(8,128)(2,1)}), bf16[64,10,2048]{2,1,0:T(8,128)(2,1)}, u32[]{:S(2)}, u32[]{:S(2)}) async-start(bf16[64,10,2048]{2,1,0:T(8,128)(2,1)} %copy.69), calls=%async_computation.2 | async-start | bytes 8388608 | tf_op jit(solution)/shard_map/all_to_all | solution.py:86
Sparse Core Ops, SparseCore 0:
  9.1 41.8 all-gather.3
  52.9 40.4 all-gather.5
  244.4 70.1 all-gather.7
  357.8 95.8 reduce-scatter.1
where the time goes:
time: 613 us; the launch traced here: 603 us
  waiting for transfers between devices  321 us (52%)
  blocking collectives  109 us (18%)
  local copies, waits for them, and re-layouts  88.1 us (14%)
  matrix products  34.3 us (6%)
  other arithmetic  23.8 us (4%)
  between operations  13.5 us (2%)
  starting transfers between devices  12.9 us (2%)
    all_to_all x1, blocking collectives, shards(): lax.all_to_all(send_buffer, 'exp', split_axis=0, concat_axis=0, tiled=True)  109 us
    reduce_scatter x1, waiting for transfers between devices, shards(): lax.psum_scatter(terms.astype(jnp.bfloat16), 'ctx', scatter_dimension=1,...  96.1 us
    all_to_all x1, waiting for transfers between devices, shards(): lax.all_to_all(summed, 'exp', split_axis=0, concat_axis=0, tiled=True)  95.9 us
    all_gather x1, waiting for transfers between devices, shards(): lax.all_gather(lax.all_to_all(send_buffer, 'exp', split_axis=0, concat_ax...  66.9 us
    all_gather x1, waiting for transfers between devices, shards(): key_part = lax.all_gather(key_rows, 'ctx', axis=1, tiled=True)  38.6 us
    all_gather x1, waiting for transfers between devices, shards(): value_part = lax.all_gather(value_rows, 'ctx', axis=1, tiled=True)  23.2 us
    convert_element_type x1, local copies, waits for them, and re-layouts, shards(): terms.astype(jnp.bfloat16)  13.8 us
    all_gather x1, local copies, waits for them, and re-layouts, shards(): lax.all_gather(lax.all_to_all(send_buffer, 'exp', split_axis=0, concat_ax...  13.6 us
  transfers between devices with their start and end apart: 5, of which 5 were waited for; matrix products, arithmetic and copies ran while one was open for 4% of the time, Pallas kernels for 0%

commit v1 on v0

--- a/solution.py
+++ b/solution.py
@@ -4,6 +4,16 @@
 from jax.sharding import PartitionSpec as P
 
 HEADS = 16
+
+
+def ctx_blocks(block):
+    count = lax.axis_size("ctx")
+    if count != 4:
+        gathered = lax.all_gather(block, "ctx", axis=0)
+        return [gathered[i] for i in range(count)]
+    far = lax.ppermute(block, "ctx", perm=[(c, c ^ 2) for c in range(count)])
+    near = lax.ppermute(jnp.stack([block, far]), "ctx", perm=[(c, c ^ 1) for c in range(count)])
+    return [block, far, near[0], near[1]]
 
 
 def shards(
@@ -23,8 +33,8 @@
     score_scale = head_size ** (-0.5)
     query_heads = queries.reshape(clip_count, row_count, head_count, head_size)
     running_max = jnp.full((clip_count, row_count, head_count), -1e30, jnp.float32)
-    key_part = lax.all_gather(key_rows, "ctx", axis=1, tiled=True)
-    value_part = lax.all_gather(value_rows, "ctx", axis=1, tiled=True)
+    key_part = jnp.concatenate(ctx_blocks(key_rows), axis=1)
+    value_part = jnp.concatenate(ctx_blocks(value_rows), axis=1)
     key_heads = key_part.reshape(clip_count, -1, head_count, head_size)
     value_heads = value_part.reshape(clip_count, -1, head_count, head_size)
     scores = (
@@ -57,32 +67,28 @@
     running_count = jnp.cumsum(one_hot, axis=0)
     slot_index = jnp.sum(running_count * one_hot, axis=1) - 1
     destination = flat_routes * capacity + slot_index
-    source_rows = jnp.repeat(normed.reshape(token_count, feature_count), top_count, axis=0)
-    send_buffer = (
-        jnp.zeros((expert_count * capacity, feature_count), jnp.bfloat16)
+    slot_token = (
+        jnp.zeros((expert_count * capacity,), jnp.int32)
         .at[destination]
-        .set(source_rows)
+        .set(jnp.arange(token_count * top_count, dtype=jnp.int32) // top_count)
     )
+    send_buffer = normed.reshape(token_count, feature_count)[slot_token]
     send_buffer = send_buffer.reshape(expert_count, capacity, feature_count)
     local_units = down_weight.shape[1]
-    portion = lax.all_gather(
-        lax.all_to_all(send_buffer, "exp", split_axis=0, concat_axis=0, tiled=True),
-        "ctx",
-        axis=1,
-        tiled=True,
-    )
+    gate_up_blocks = ctx_blocks(gate_up_weight[0].reshape(feature_count, 2 * local_units))
+    down_blocks = ctx_blocks(down_weight[0])
+    portion = lax.all_to_all(send_buffer, "exp", split_axis=0, concat_axis=0, tiled=True)
     flattened = portion.reshape(-1, feature_count)
-    gate_and_up = jnp.dot(
-        flattened,
-        gate_up_weight[0].reshape(feature_count, 2 * local_units),
-        preferred_element_type=jnp.float32,
-    )
-    hidden = (jax.nn.silu(gate_and_up[:, :local_units]) * gate_and_up[:, local_units:]).astype(
-        jnp.bfloat16
-    )
-    projected = jnp.dot(hidden, down_weight[0], preferred_element_type=jnp.float32)
-    terms = projected.reshape(portion.shape[0], portion.shape[1], feature_count)
-    summed = lax.psum_scatter(terms.astype(jnp.bfloat16), "ctx", scatter_dimension=1, tiled=True)
+    summed = None
+    for gate_up_block, down_block in zip(gate_up_blocks, down_blocks):
+        gate_and_up = jnp.dot(flattened, gate_up_block, preferred_element_type=jnp.float32)
+        hidden = (
+            jax.nn.silu(gate_and_up[:, :local_units]) * gate_and_up[:, local_units:]
+        ).astype(jnp.bfloat16)
+        group_part = jnp.dot(hidden, down_block, preferred_element_type=jnp.float32)
+        group_part = group_part.astype(jnp.bfloat16).astype(jnp.float32)
+        summed = group_part if summed is None else summed + group_part
+    summed = summed.astype(jnp.bfloat16).reshape(portion.shape)
     returned = lax.all_to_all(summed, "exp", split_axis=0, concat_axis=0, tiled=True)
     expert_out = returned.reshape(-1, feature_count)[destination]
     expert_out = expert_out.reshape(token_count, top_count, feature_count).astype(jnp.float32)

time: 613 us -> 417 us (0.68)
  blocking collectives: 109 us -> 0 us
  waiting for transfers between devices: 321 us -> 250 us
  local copies, waits for them, and re-layouts: 88.1 us -> 57.8 us
  starting transfers between devices: 12.9 us -> 32.5 us
  between operations: 13.5 us -> 0.83 us
  other arithmetic: 23.8 us -> 31.6 us
    ppermute x0 -> x8, waiting for transfers between devices: none -> 153 us  [the longest x4 153 us: ctx_blocks(): far = lax.ppermute(block, 'ctx', perm=[(c, c ^ 2) for c in range(count)])]
    all_gather x3 -> x0, waiting for transfers between devices: 129 us -> none  [the longest x1 66.9 us: shards(): lax.all_gather(lax.all_to_all(send_buffer, 'exp', split_axis=0, concat_ax...]
    all_to_all x1 -> x0, blocking collectives: 109 us -> none  [shards(): lax.all_to_all(send_buffer, 'exp', split_axis=0, concat_axis=0, tiled=True)]
    reduce_scatter x1 -> x0, waiting for transfers between devices: 96.1 us -> none  [shards(): lax.psum_scatter(terms.astype(jnp.bfloat16), 'ctx', scatter_dimension=1,...]
    all_gather x2 -> x0, local copies, waits for them, and re-layouts: 20 us -> none  [the longest x1 13.6 us: shards(): lax.all_gather(lax.all_to_all(send_buffer, 'exp', split_axis=0, concat_ax...]
    convert_element_type x1 -> x0, local copies, waits for them, and re-layouts: 13.8 us -> none  [shards(): terms.astype(jnp.bfloat16)]
    all_to_all x0 -> x1, starting transfers between devices: none -> 13.1 us  [shards(): lax.all_to_all(send_buffer, 'exp', split_axis=0, concat_axis=0, tiled=True)]
    another operation x2 -> x6, other arithmetic: 1.24 us -> 11.9 us  [the longest x4 10.7 us: ctx_blocks(): jnp.stack([block, far])]
  transfers between devices with their start and end apart: 5 -> 10, of which waited for: 5 -> 5; matrix products, arithmetic and copies ran while one was open for 4% -> 14% of each run, Pallas kernels for 0% -> 0%
where the time goes in v1:
time: 417 us; the launch traced here: 412 us
  waiting for transfers between devices  250 us (60%)
  local copies, waits for them, and re-layouts  57.8 us (14%)
  matrix products  39.1 us (9%)
  starting transfers between devices  32.5 us (8%)
  other arithmetic  31.6 us (8%)
    ppermute x4, waiting for transfers between devices, ctx_blocks(): far = lax.ppermute(block, 'ctx', perm=[(c, c ^ 2) for c in range(count)])  153 us
    all_to_all x1, waiting for transfers between devices, shards(): lax.all_to_all(summed, 'exp', split_axis=0, concat_axis=0, tiled=True)  96.7 us
    all_to_all x1, starting transfers between devices, shards(): lax.all_to_all(summed, 'exp', split_axis=0, concat_axis=0, tiled=True)  13.3 us
    all_to_all x1, starting transfers between devices, shards(): lax.all_to_all(send_buffer, 'exp', split_axis=0, concat_axis=0, tiled=True)  13.1 us
    dot_general x4, matrix products, shards(): jnp.dot(flattened, gate_up_block, preferred_element_type=jnp.float32)  12.6 us
    another operation x4, other arithmetic, ctx_blocks(): jnp.stack([block, far])  10.7 us
    dot_general x1, matrix products, shards(): jnp.einsum('cqhk,ckhd->cqhd', expo.astype(jnp.bfloat16), value_heads, pre...  10.1 us
    dot_general x1, matrix products, shards(): jnp.einsum('cqhd,ckhd->cqhk', query_heads, key_heads, preferred_element_t...  9.75 us
  transfers between devices with their start and end apart: 10, of which 5 were waited for; matrix products, arithmetic and copies ran while one was open for 14% of the time, Pallas kernels for 0%

profile of v1, /device:TPU:4, one launch (start us, length us, event | category | flops | bytes accessed | tf_op | source)
XLA Modules:
  0.0 411.8 jit_solution(18258981865370532754)
XLA Ops:
  3.8 24.2 %collective-permute-done.2 = bf16[1,256,2048]{1,2,0:T(8,128)(2,1)S(1)} collective-permute-done((bf16[1,256,2048]{1,2,0:T(8,128)(2,1)S(1)}, bf16[1,256,2048]{1,2,0:T(8,128)(2,1)S(1)}, u32[]{:S(2)}, u32[]{:S(2)}) %collective-permute-start.2) | collective-permute-done | bytes 1048608 | tf_op jit(solution)/shard_map/ppermute | solution.py:14
  37.2 19.5 %collective-permute-done = bf16[1,256,2048]{2,1,0:T(8,128)(2,1)} collective-permute-done((bf16[1,256,2048]{2,1,0:T(8,128)(2,1)S(1)}, bf16[1,256,2048]{2,1,0:T(8,128)(2,1)}, u32[]{:S(2)}, u32[]{:S(2)}) %collective-permute-start) | collective-permute-done | bytes 1048608 | tf_op jit(solution)/shard_map/ppermute | solution.py:14
  69.4 9.7 %bitcast_reduce_fusion = (f32[256,16]{0,1:T(8,128)S(1)}, f32[16,1024,256]{2,1,0:T(8,128)}) fusion(bf16[256,16,128]{2,1,0:T(8,128)(2,1)} %bitcast.111, bf16[1,256,16,128]{3,1,2,0:T(8,128)(2,1)S(1)} %copy.28, bf16[1,256,16,128]{3,1,2,0:T(8,128)(2,1)} %copy.27, bf16[1,256,16,128]{3,1,2,0:T(8,128)(2,1)} %copy.26, bf16[1,256,16,128]{3,1,2,0:T(8,128)(2,1)S(1)} %copy-done.6), kind=kOutput, calls=%fused_computation.4 | convolution fusion | flops 1098903552 | bytes 22036480 | tf_op jit(solution)/shard_map/cqhd,ckhd->cqhk/dot_general | solution.py:41
  82.7 8.6 %fusion.1 = f32[256,16]{0,1:T(8,128)S(1)} fusion(f32[16,1024,256]{2,1,0:T(8,128)} %get-tuple-element.12, f32[256,16]{0,1:T(8,128)S(1)} %broadcast_maximum_fusion), kind=kLoop, calls=%fused_computation.6 | loop fusion | flops 12578816 | bytes 16809984 | tf_op jit(solution)/shard_map/reduce_sum | solution.py:46
  91.4 10.1 %bitcast_divide_fusion = f32[1,256,16,128]{1,3,2,0:T(8,128)} fusion(f32[256,16]{0,1:T(8,128)S(1)} %fusion.1, f32[16,1024,256]{2,1,0:T(8,128)} %get-tuple-element.12, f32[256,16]{0,1:T(8,128)S(1)} %broadcast_maximum_fusion, bf16[1,256,16,128]{1,3,2,0:T(8,128)(2,1)} %bitcast.114, bf16[1,256,16,128]{1,3,2,0:T(8,128)(2,1)S(1)} %bitcast.113, ...), kind=kOutput, calls=%fused_computation.48 | convolution fusion | flops 1103626240 | bytes 23101440 | tf_op jit(solution)/shard_map/cqhk,ckhd->cqhd/dot_general | solution.py:47
  105.2 4.1 gather_fusion
  109.3 5.6 %reshape.146 = bf16[64,10,2048]{2,1,0:T(8,128)(2,1)} reshape(bf16[640,2048]{1,0:T(8,128)(2,1)} %gather_fusion) | data formatting | bytes 5242880 | tf_op jit(solution)/shard_map/reshape | solution.py:76
  114.9 13.1 %all-to-all-start = ((bf16[64,10,2048]{2,1,0:T(8,128)(2,1)}), bf16[64,10,2048]{2,1,0:T(8,128)(2,1)}, u32[]{:S(2)}, u32[]{:S(2)}) async-start(bf16[64,10,2048]{2,1,0:T(8,128)(2,1)} %reshape.146), calls=%async_computation | async-start | bytes 8388608 | tf_op jit(solution)/shard_map/all_to_all | solution.py:80
  133.2 85.2 %collective-permute-done.4 = bf16[2048,512]{1,0:T(8,128)(2,1)} collective-permute-done((bf16[2048,512]{1,0:T(8,128)(2,1)}, bf16[2048,512]{1,0:T(8,128)(2,1)}, u32[]{:S(2)}, u32[]{:S(2)}) %collective-permute-start.4) | collective-permute-done | bytes 2097184 | tf_op jit(solution)/shard_map/ppermute | solution.py:14
  218.4 4.6 %pad_maximum_fusion = bf16[2,2048,512]{2,1,0:T(8,128)(2,1)} fusion(bf16[1,2048,512]{2,1,0:T(8,128)(2,1)} %bitcast.27, bf16[1,2048,512]{2,1,0:T(8,128)(2,1)} %stack_reshape_squeeze.3), kind=kLoop, calls=%fused_computation.28 | loop fusion | flops 2097152 | bytes 8388608 | tf_op jit(solution)/shard_map/stack | solution.py:15
  225.8 24.3 %collective-permute-done.5 = bf16[256,2048]{1,0:T(8,128)(2,1)S(1)} collective-permute-done((bf16[256,2048]{1,0:T(8,128)(2,1)S(1)}, bf16[256,2048]{1,0:T(8,128)(2,1)S(1)}, u32[]{:S(2)}, u32[]{:S(2)}) %collective-permute-start.5) | collective-permute-done | bytes 1048608 | tf_op jit(solution)/shard_map/ppermute | solution.py:14
  251.9 4.1 reshape.147
  256.0 3.2 fusion.61
  260.1 3.2 fusion.62
  264.2 3.1 fusion.26
  267.3 3.1 fusion.25
  272.5 2.8 add_convert_fusion
  275.3 2.8 reshape.148
  278.1 13.3 %all-to-all-start.1 = ((bf16[64,10,2048]{2,1,0:T(8,128)(2,1)}), bf16[64,10,2048]{2,1,0:T(8,128)(2,1)}, u32[]{:S(2)}, u32[]{:S(2)}) async-start(bf16[64,10,2048]{2,1,0:T(8,128)(2,1)} %reshape.148), calls=%async_computation.1 | async-start | bytes 8388608 | tf_op jit(solution)/shard_map/all_to_all | solution.py:92
  291.5 96.7 %all-to-all-done.1 = bf16[64,10,2048]{2,1,0:T(8,128)(2,1)} async-done(((bf16[64,10,2048]{2,1,0:T(8,128)(2,1)}), bf16[64,10,2048]{2,1,0:T(8,128)(2,1)}, u32[]{:S(2)}, u32[]{:S(2)}) %all-to-all-start.1) | async-done | bytes 2621472 | tf_op jit(solution)/shard_map/all_to_all | solution.py:92
  388.2 4.1 reshape.149
  392.3 3.3 gather_fusion.1
  395.6 5.4 %reshape.150 = f32[256,2,2048]{2,1,0:T(2,128)} reshape(bf16[512,2048]{1,0:T(8,128)(2,1)} %gather_fusion.1) | data formatting | bytes 6291456 | tf_op jit(solution)/shard_map/convert_element_type | solution.py:94
  401.1 9.0 %multiply_reduce_fusion = f32[256,2048]{1,0:T(8,128)S(1)} fusion(f32[256,2,2048]{2,1,0:T(2,128)} %reshape.150, f32[256,2]{1,0:T(8,128)S(1)} %copy.32), kind=kLoop, calls=%fused_computation.29 | loop fusion | flops 1572864 | bytes 6293504 | tf_op jit(solution)/shard_map/reduce_sum | solution.py:95
  (89 shorter events, 47.8 us)
Async XLA Ops:
  1.5 28.0 %copy-start.3 = (bf16[1,256,2048]{2,1,0:T(8,128)(2,1)S(1)}, bf16[1,256,2048]{2,1,0:T(8,128)(2,1)}, u32[]{:S(2)}) copy-start(bf16[1,256,2048]{2,1,0:T(8,128)(2,1)} %param.11) | copy-start | bytes 3145732
  1.5 26.5 %collective-permute-start.2 = (bf16[1,256,2048]{1,2,0:T(8,128)(2,1)S(1)}, bf16[1,256,2048]{1,2,0:T(8,128)(2,1)S(1)}, u32[]{:S(2)}, u32[]{:S(2)}) collective-permute-start(bf16[1,256,2048]{1,2,0:T(8,128)(2,1)S(1)} %copy.22), channel_id=1, source_target_pairs={{0,128},{64,192},{128,0},{192,64},{1,129},{65,193},{129,1},{193,65... | collective-permute-start | bytes 3145736 | tf_op jit(solution)/shard_map/ppermute | solution.py:14
  28.0 3.1 copy-start.13
  29.5 36.2 %collective-permute-start.3 = (bf16[2,1,256,2048]{2,3,1,0:T(8,128)(2,1)}, bf16[2,1,256,2048]{2,3,1,0:T(8,128)(2,1)}, u32[]{:S(2)}, u32[]{:S(2)}) collective-permute-start(bf16[2,1,256,2048]{2,3,1,0:T(8,128)(2,1)} %pad_maximum_fusion.2), channel_id=1, source_target_pairs={{0,64},{64,0},{128,192},{192,128},{1,65},{65,1},{129,193},{193,129... | collective-permute-start | bytes 6291464 | tf_op jit(solution)/shard_map/ppermute | solution.py:15
  29.5 27.2 %collective-permute-start = (bf16[1,256,2048]{2,1,0:T(8,128)(2,1)S(1)}, bf16[1,256,2048]{2,1,0:T(8,128)(2,1)}, u32[]{:S(2)}, u32[]{:S(2)}) collective-permute-start(bf16[1,256,2048]{2,1,0:T(8,128)(2,1)S(1)} %copy-done.3), channel_id=1, source_target_pairs={{0,128},{64,192},{128,0},{192,64},{1,129},{65,193},{129,1},{193,65... | collective-permute-start | bytes 3145736 | tf_op jit(solution)/shard_map/ppermute | solution.py:14
  59.5 19.7 %collective-permute-start.1 = (bf16[2,1,256,2048]{3,2,1,0:T(8,128)(2,1)}, bf16[2,1,256,2048]{3,2,1,0:T(8,128)(2,1)}, u32[]{:S(2)}, u32[]{:S(2)}) collective-permute-start(bf16[2,1,256,2048]{3,2,1,0:T(8,128)(2,1)} %pad_maximum_fusion.1), channel_id=1, source_target_pairs={{0,64},{64,0},{128,192},{192,128},{1,65},{65,1},{129,193},{193,129... | collective-permute-start | bytes 6291464 | tf_op jit(solution)/shard_map/ppermute | solution.py:15
  67.4 2.0 copy-start.6
  82.7 8.7 %copy-start.5 = (bf16[1,256,2048]{1,2,0:T(8,128)(2,1)S(1)}, bf16[1,256,2048]{1,2,0:T(8,128)(2,1)}, u32[]{:S(2)}) copy-start(bf16[1,256,2048]{1,2,0:T(8,128)(2,1)} %copy.18) | copy-start | bytes 3145732
  82.7 8.7 %copy-start.7 = (bf16[1,256,2048]{1,2,0:T(8,128)(2,1)S(1)}, bf16[1,256,2048]{1,2,0:T(8,128)(2,1)}, u32[]{:S(2)}) copy-start(bf16[1,256,2048]{1,2,0:T(8,128)(2,1)} %copy.19) | copy-start | bytes 3145732
  101.5 2.0 copy-start.4
  103.5 1.4 copy-start.12
  114.9 13.1 %copy-start.2 = (bf16[1,2048,2,256]{3,2,1,0:T(2,128)(2,1)S(1)}, bf16[1,2048,2,256]{3,2,1,0:T(2,128)(2,1)}, u32[]{:S(2)}) copy-start(bf16[1,2048,2,256]{3,2,1,0:T(2,128)(2,1)} %param.16) | copy-start | bytes 6291460
  114.9 137.0 %all-to-all-start = ((bf16[64,10,2048]{2,1,0:T(8,128)(2,1)}), bf16[64,10,2048]{2,1,0:T(8,128)(2,1)}, u32[]{:S(2)}, u32[]{:S(2)}) async-start(bf16[64,10,2048]{2,1,0:T(8,128)(2,1)} %reshape.146), calls=%async_computation | async-start | bytes 8388608 | tf_op jit(solution)/shard_map/all_to_all | solution.py:80
  129.8 88.6 %collective-permute-start.4 = (bf16[2048,512]{1,0:T(8,128)(2,1)}, bf16[2048,512]{1,0:T(8,128)(2,1)}, u32[]{:S(2)}, u32[]{:S(2)}) collective-permute-start(bf16[2048,512]{1,0:T(8,128)(2,1)} %bitcast.42), channel_id=1, source_target_pairs={{0,128},{64,192},{128,0},{192,64},{1,129},{65,193},{129,1},{193,65... | collective-permute-start | bytes 6291464 | tf_op jit(solution)/shard_map/ppermute | solution.py:14
  218.4 4.7 %copy-start.8 = (bf16[1,256,2048]{2,1,0:T(8,128)(2,1)S(1)}, bf16[1,256,2048]{2,1,0:T(8,128)(2,1)}, u32[]{:S(2)}) copy-start(bf16[1,256,2048]{2,1,0:T(8,128)(2,1)} %param.17) | copy-start | bytes 3145732
  223.0 41.1 %collective-permute-start.6 = (bf16[2,2048,512]{2,1,0:T(8,128)(2,1)}, bf16[2,2048,512]{2,1,0:T(8,128)(2,1)}, u32[]{:S(2)}, u32[]{:S(2)}) collective-permute-start(bf16[2,2048,512]{2,1,0:T(8,128)(2,1)} %pad_maximum_fusion), channel_id=1, source_target_pairs={{0,64},{64,0},{128,192},{192,128},{1,65},{65,1},{129,193},{193,129... | collective-permute-start | bytes 12582920 | tf_op jit(solution)/shard_map/ppermute | solution.py:15
  223.0 27.1 %collective-permute-start.5 = (bf16[256,2048]{1,0:T(8,128)(2,1)S(1)}, bf16[256,2048]{1,0:T(8,128)(2,1)S(1)}, u32[]{:S(2)}, u32[]{:S(2)}) collective-permute-start(bf16[256,2048]{1,0:T(8,128)(2,1)S(1)} %bitcast.115), channel_id=1, source_target_pairs={{0,128},{64,192},{128,0},{192,64},{1,129},{65,193},{129,1},{193,65... | collective-permute-start | bytes 3145736 | tf_op jit(solution)/shard_map/ppermute | solution.py:14
  250.1 1.7 copy-start.10
  251.8 18.5 %collective-permute-start.7 = (bf16[2,256,2048]{2,1,0:T(8,128)(2,1)}, bf16[2,256,2048]{2,1,0:T(8,128)(2,1)}, u32[]{:S(2)}, u32[]{:S(2)}) collective-permute-start(bf16[2,256,2048]{2,1,0:T(8,128)(2,1)} %pad_maximum_fusion.3), channel_id=1, source_target_pairs={{0,64},{64,0},{128,192},{192,128},{1,65},{65,1},{129,193},{193,129... | collective-permute-start | bytes 6291464 | tf_op jit(solution)/shard_map/ppermute | solution.py:15
  256.0 3.2 copy-start.9
  260.1 3.2 copy-start.11
  278.1 13.3 %copy-start.14 = (f32[1,256,2]{1,2,0:T(2,128)S(1)}, f32[1,256,2]{1,2,0:T(2,128)}, u32[]{:S(2)}) copy-start(f32[1,256,2]{1,2,0:T(2,128)} %param.15) | copy-start | bytes 6148
  278.1 110.2 %all-to-all-start.1 = ((bf16[64,10,2048]{2,1,0:T(8,128)(2,1)}), bf16[64,10,2048]{2,1,0:T(8,128)(2,1)}, u32[]{:S(2)}, u32[]{:S(2)}) async-start(bf16[64,10,2048]{2,1,0:T(8,128)(2,1)} %reshape.148), calls=%async_computation.1 | async-start | bytes 8388608 | tf_op jit(solution)/shard_map/all_to_all | solution.py:92
  401.1 9.0 %copy-start.1 = (bf16[1,256,2048]{2,1,0:T(8,128)(2,1)S(1)}, bf16[1,256,2048]{2,1,0:T(8,128)(2,1)}, u32[]{:S(2)}) copy-start(bf16[1,256,2048]{2,1,0:T(8,128)(2,1)} %copy-done) | copy-start | bytes 3145732
  (1 other events, 1.0 us)

commit v2 on v1

--- a/solution.py
+++ b/solution.py
@@ -6,13 +6,14 @@
 HEADS = 16
 
 
-def ctx_blocks(block):
-    count = lax.axis_size("ctx")
-    if count != 4:
-        gathered = lax.all_gather(block, "ctx", axis=0)
-        return [gathered[i] for i in range(count)]
-    far = lax.ppermute(block, "ctx", perm=[(c, c ^ 2) for c in range(count)])
-    near = lax.ppermute(jnp.stack([block, far]), "ctx", perm=[(c, c ^ 1) for c in range(count)])
+def far_block(block, after=None):
+    if after is not None:
+        block, _ = lax.optimization_barrier((block, after))
+    return lax.ppermute(block, "ctx", perm=[(c, c ^ 2) for c in range(4)])
+
+
+def near_blocks(block, far):
+    near = lax.ppermute(jnp.stack([block, far]), "ctx", perm=[(c, c ^ 1) for c in range(4)])
     return [block, far, near[0], near[1]]
 
 
@@ -33,8 +34,15 @@
     score_scale = head_size ** (-0.5)
     query_heads = queries.reshape(clip_count, row_count, head_count, head_size)
     running_max = jnp.full((clip_count, row_count, head_count), -1e30, jnp.float32)
-    key_part = jnp.concatenate(ctx_blocks(key_rows), axis=1)
-    value_part = jnp.concatenate(ctx_blocks(value_rows), axis=1)
+    local_units = down_weight.shape[1]
+    gate_up_local = gate_up_weight[0].reshape(feature_count, 2 * local_units)
+    down_local = down_weight[0]
+    key_far = far_block(key_rows)
+    value_far = far_block(value_rows, key_far)
+    gate_up_far = far_block(gate_up_local, value_far)
+    down_far = far_block(down_local, gate_up_far)
+    key_part = jnp.concatenate(near_blocks(key_rows, key_far), axis=1)
+    value_part = jnp.concatenate(near_blocks(value_rows, value_far), axis=1)
     key_heads = key_part.reshape(clip_count, -1, head_count, head_size)
     value_heads = value_part.reshape(clip_count, -1, head_count, head_size)
     scores = (
@@ -72,11 +80,11 @@
         .at[destination]
         .set(jnp.arange(token_count * top_count, dtype=jnp.int32) // top_count)
     )
+    normed, gate_up_far, down_far = lax.optimization_barrier((normed, gate_up_far, down_far))
     send_buffer = normed.reshape(token_count, feature_count)[slot_token]
-    send_buffer = send_buffer.reshape(expert_count, capacity, feature_count)
-    local_units = down_weight.shape[1]
-    gate_up_blocks = ctx_blocks(gate_up_weight[0].reshape(feature_count, 2 * local_units))
-    down_blocks = ctx_blocks(down_weight[0])
+    send_buffer = send_buffer.reshape(expert_count, capacity * feature_count)
+    gate_up_blocks = near_blocks(gate_up_local, gate_up_far)
+    down_blocks = near_blocks(down_local, down_far)
     portion = lax.all_to_all(send_buffer, "exp", split_axis=0, concat_axis=0, tiled=True)
     flattened = portion.reshape(-1, feature_count)
     summed = None

time: 417 us -> 449 us (1.077)
  waiting for transfers between devices: 250 us -> 182 us
  other arithmetic: 31.6 us -> 97.6 us
  local copies, waits for them, and re-layouts: 57.8 us -> 96.3 us
  starting transfers between devices: 32.5 us -> 23.7 us
    ppermute x8, waiting for transfers between devices: 153 us -> 72 us  [the longest x4 72 us: far_block(): return lax.ppermute(block, 'ctx', perm=[(c, c ^ 2) for c in range(4)])]
    all_to_all x0 -> x4, other arithmetic: none -> 64.8 us  [the longest x2 33.2 us: shards(): lax.all_to_all(summed, 'exp', split_axis=0, concat_axis=0, tiled=True)]
    all_to_all x1, waiting for transfers between devices: 0.01 us -> 48.6 us  [shards(): lax.all_to_all(send_buffer, 'exp', split_axis=0, concat_axis=0, tiled=True)]
    all_to_all x1, waiting for transfers between devices: 96.7 us -> 61.2 us  [shards(): lax.all_to_all(summed, 'exp', split_axis=0, concat_axis=0, tiled=True)]
    unnamed x35 -> x37, local copies, waits for them, and re-layouts: 8.16 us -> 30.9 us
    all_to_all x0 -> x3, local copies, waits for them, and re-layouts: none -> 20.4 us  [the longest x2 12.3 us: shards(): lax.all_to_all(send_buffer, 'exp', split_axis=0, concat_axis=0, tiled=True)]
    reshape x2 -> x0, local copies, waits for them, and re-layouts: 8.33 us -> none  [the longest x1 5.56 us: shards(): send_buffer = send_buffer.reshape(expert_count, capacity, feature_count)]
    all_to_all x1, starting transfers between devices: 13.3 us -> 6.3 us  [shards(): lax.all_to_all(summed, 'exp', split_axis=0, concat_axis=0, tiled=True)]
  transfers between devices with their start and end apart: 10 -> 10, of which waited for: 5 -> 6; matrix products, arithmetic and copies ran while one was open for 14% -> 26% of each run, Pallas kernels for 0% -> 0%
where the time goes in v2:
time: 449 us; the launch traced here: 442 us
  waiting for transfers between devices  182 us (41%)
  other arithmetic  97.6 us (22%)
  local copies, waits for them, and re-layouts  96.3 us (21%)
  matrix products  42.1 us (9%)
  starting transfers between devices  23.7 us (5%)
    ppermute x4, waiting for transfers between devices, far_block(): return lax.ppermute(block, 'ctx', perm=[(c, c ^ 2) for c in range(4)])  72 us
    all_to_all x1, waiting for transfers between devices, shards(): lax.all_to_all(summed, 'exp', split_axis=0, concat_axis=0, tiled=True)  61.2 us
    all_to_all x1, waiting for transfers between devices, shards(): lax.all_to_all(send_buffer, 'exp', split_axis=0, concat_axis=0, tiled=True)  48.6 us
    all_to_all x2, other arithmetic, shards(): lax.all_to_all(summed, 'exp', split_axis=0, concat_axis=0, tiled=True)  33.2 us
    all_to_all x2, other arithmetic, shards(): lax.all_to_all(send_buffer, 'exp', split_axis=0, concat_axis=0, tiled=True)  31.6 us
    unnamed x37, local copies, waits for them, and re-layouts  30.9 us
    dot_general x4, matrix products, shards(): jnp.dot(flattened, gate_up_block, preferred_element_type=jnp.float32)  13.3 us
    all_to_all x1, starting transfers between devices, shards(): lax.all_to_all(send_buffer, 'exp', split_axis=0, concat_axis=0, tiled=True)  12.7 us
  transfers between devices with their start and end apart: 10, of which 6 were waited for; matrix products, arithmetic and copies ran while one was open for 26% of the time, Pallas kernels for 0%

profile of v2, /device:TPU:4, one launch (start us, length us, event | category | flops | bytes accessed | tf_op | source)
XLA Modules:
  0.0 442.3 jit_solution(7152388930009791485)
XLA Ops:
  3.8 24.2 %collective-permute-done = bf16[1,256,2048]{1,2,0:T(8,128)(2,1)S(1)} collective-permute-done((bf16[1,256,2048]{1,2,0:T(8,128)(2,1)S(1)}, bf16[1,256,2048]{1,2,0:T(8,128)(2,1)S(1)}, u32[]{:S(2)}, u32[]{:S(2)}) %collective-permute-start) | collective-permute-done | bytes 1048608 | tf_op jit(solution)/shard_map/ppermute | solution.py:12
  45.0 14.5 %collective-permute-done.1 = bf16[1,256,2048]{2,1,0:T(8,128)(2,1)} collective-permute-done((bf16[1,256,2048]{2,1,0:T(8,128)(2,1)}, bf16[1,256,2048]{2,1,0:T(8,128)(2,1)}, u32[]{:S(2)}, u32[]{:S(2)}) %collective-permute-start.1) | collective-permute-done | bytes 1048608 | tf_op jit(solution)/shard_map/ppermute | solution.py:12
  69.0 9.8 %bitcast_reduce_fusion = (f32[256,16]{0,1:T(8,128)S(1)}, f32[16,1024,256]{2,1,0:T(8,128)}) fusion(bf16[256,16,128]{2,1,0:T(8,128)(2,1)} %bitcast.110, bf16[1,256,16,128]{3,1,2,0:T(8,128)(2,1)S(1)} %copy.68, bf16[1,256,16,128]{3,1,2,0:T(8,128)(2,1)} %copy.67, bf16[1,256,16,128]{3,1,2,0:T(8,128)(2,1)} %copy.66, bf16[1,256,16,128]{3,1,2,0:T(8,128)(2,1)S(1)} %copy-done.8), kind=kOutput, calls=%fused_computation.4 | convolution fusion | flops 1098903552 | bytes 22036480 | tf_op jit(solution)/shard_map/cqhd,ckhd->cqhk/dot_general | solution.py:49
  78.8 8.5 %fusion.1 = f32[256,16]{0,1:T(8,128)S(1)} fusion(f32[16,1024,256]{2,1,0:T(8,128)} %get-tuple-element.24, f32[256,16]{0,1:T(8,128)S(1)} %broadcast_maximum_fusion), kind=kLoop, calls=%fused_computation.6 | loop fusion | flops 12578816 | bytes 16809984 | tf_op jit(solution)/shard_map/reduce_sum | solution.py:54
  90.8 11.0 %bitcast_divide_fusion = f32[1,256,16,128]{1,3,2,0:T(8,128)} fusion(f32[256,16]{0,1:T(8,128)S(1)} %fusion.1, f32[16,1024,256]{2,1,0:T(8,128)} %get-tuple-element.24, f32[256,16]{0,1:T(8,128)S(1)} %broadcast_maximum_fusion, bf16[1,256,16,128]{1,3,2,0:T(8,128)(2,1)S(1)} %bitcast.113, bf16[1,256,16,128]{1,3,2,0:T(8,128)(2,1)} %bitcast.112, ...), kind=kOutput, calls=%fused_computation.48 | convolution fusion | flops 1103626240 | bytes 23101440 | tf_op jit(solution)/shard_map/cqhk,ckhd->cqhd/dot_general | solution.py:55
  103.9 8.7 %collective-permute-done.4 = bf16[2048,512]{1,0:T(8,128)(2,1)} collective-permute-done((bf16[2048,512]{1,0:T(8,128)(2,1)}, bf16[2048,512]{1,0:T(8,128)(2,1)}, u32[]{:S(2)}, u32[]{:S(2)}) %collective-permute-start.4) | collective-permute-done | bytes 2097184 | tf_op jit(solution)/shard_map/ppermute | solution.py:12
  114.8 24.6 %collective-permute-done.5 = bf16[256,2048]{1,0:T(8,128)(2,1)} collective-permute-done((bf16[256,2048]{1,0:T(8,128)(2,1)}, bf16[256,2048]{1,0:T(8,128)(2,1)}, u32[]{:S(2)}, u32[]{:S(2)}) %collective-permute-start.5) | collective-permute-done | bytes 1048608 | tf_op jit(solution)/shard_map/ppermute | solution.py:12
  143.5 11.7 %all_to_all.16 = bf16[64,1,20480]{2,1,0:T(2,128)(2,1)} reshape(bf16[640,2048]{1,0:T(8,128)(2,1)} %gather_fusion) | data formatting | bytes 5242880 | tf_op jit(solution)/shard_map/all_to_all | solution.py:88
  155.8 16.1 %reduce.7 = bf16[64,20480]{1,0:T(8,128)(2,1)S(1)} reduce(bf16[64,1,20480]{2,1,0:T(2,128)(2,1)} %all_to_all.16, bf16[]{:T(256)} %broadcast.128), dimensions={1}, to_apply=%all_to_all.16.reduce_sub_computation | reduce | bytes 5242882 | tf_op jit(solution)/shard_map/all_to_all | solution.py:88
  175.0 12.7 %all-to-all-start = ((bf16[64,2,10240]{2,1,0:T(2,128)(2,1)}), bf16[64,2,10240]{2,1,0:T(2,128)(2,1)S(1)}, u32[]{:S(2)}, u32[]{:S(2)}) async-start(bf16[64,2,10240]{2,1,0:T(2,128)(2,1)} %reshape.183), calls=%async_computation | async-start | bytes 5242880 | tf_op jit(solution)/shard_map/all_to_all | solution.py:88
  192.2 4.7 %pad_maximum_fusion = bf16[2,2048,512]{2,1,0:T(8,128)(2,1)} fusion(bf16[1,2048,512]{2,1,0:T(8,128)(2,1)} %bitcast.27, bf16[1,2048,512]{2,1,0:T(8,128)(2,1)} %stack_reshape_squeeze.3), kind=kLoop, calls=%fused_computation.28 | loop fusion | flops 2097152 | bytes 8388608 | tf_op jit(solution)/shard_map/stack | solution.py:16
  200.5 48.6 %all-to-all-done = bf16[64,2,10240]{2,1,0:T(2,128)(2,1)S(1)} async-done(((bf16[64,2,10240]{2,1,0:T(2,128)(2,1)}), bf16[64,2,10240]{2,1,0:T(2,128)(2,1)S(1)}, u32[]{:S(2)}, u32[]{:S(2)}) %all-to-all-start) | async-done | bytes 2621472 | tf_op jit(solution)/shard_map/all_to_all | solution.py:88
  249.2 7.2 %reshape.184 = bf16[64,1,20480]{2,1,0:T(2,128)(2,1)} reshape(bf16[64,2,10240]{2,1,0:T(2,128)(2,1)S(1)} %all-to-all-done) | data formatting | bytes 5242880
  256.4 15.5 %reduce.4 = bf16[64,20480]{1,0:T(8,128)(2,1)S(1)} reduce(bf16[64,1,20480]{2,1,0:T(2,128)(2,1)} %reshape.184, bf16[]{:T(256)} %constant.59), dimensions={1}, to_apply=%all_to_all.13.reduce_sub_computation | reduce | bytes 5242882 | tf_op jit(solution)/shard_map/all_to_all | solution.py:88
  271.8 4.9 %reshape.150 = bf16[640,2048]{1,0:T(8,128)(2,1)} reshape(bf16[64,20480]{1,0:T(8,128)(2,1)S(1)} %reduce.4) | data formatting | bytes 5242880 | tf_op jit(solution)/shard_map/reshape | solution.py:89
  298.1 8.1 %all_to_all.17 = bf16[64,1,20480]{2,1,0:T(2,128)(2,1)} reshape(bf16[640,2048]{1,0:T(8,128)(2,1)S(1)} %add_convert_fusion) | data formatting | bytes 5242880 | tf_op jit(solution)/shard_map/all_to_all | solution.py:100
  306.3 16.3 %reduce.8 = bf16[64,20480]{1,0:T(8,128)(2,1)S(1)} reduce(bf16[64,1,20480]{2,1,0:T(2,128)(2,1)} %all_to_all.17, bf16[]{:T(256)} %broadcast.128), dimensions={1}, to_apply=%all_to_all.17.reduce_sub_computation | reduce | bytes 5242882 | tf_op jit(solution)/shard_map/all_to_all | solution.py:100
  325.7 6.3 %all-to-all-start.1 = ((bf16[64,2,10240]{2,1,0:T(2,128)(2,1)}), bf16[64,2,10240]{2,1,0:T(2,128)(2,1)S(1)}, u32[]{:S(2)}, u32[]{:S(2)}) async-start(bf16[64,2,10240]{2,1,0:T(2,128)(2,1)} %reshape.185), calls=%async_computation.1 | async-start | bytes 5242880 | tf_op jit(solution)/shard_map/all_to_all | solution.py:100
  332.2 61.2 %all-to-all-done.1 = bf16[64,2,10240]{2,1,0:T(2,128)(2,1)S(1)} async-done(((bf16[64,2,10240]{2,1,0:T(2,128)(2,1)}), bf16[64,2,10240]{2,1,0:T(2,128)(2,1)S(1)}, u32[]{:S(2)}, u32[]{:S(2)}) %all-to-all-start.1) | async-done | bytes 2621472 | tf_op jit(solution)/shard_map/all_to_all | solution.py:100
  393.4 7.2 %reshape.186 = bf16[64,1,20480]{2,1,0:T(2,128)(2,1)} reshape(bf16[64,2,10240]{2,1,0:T(2,128)(2,1)S(1)} %all-to-all-done.1) | data formatting | bytes 5242880
  400.6 17.0 %reduce.5 = bf16[64,20480]{1,0:T(8,128)(2,1)} reduce(bf16[64,1,20480]{2,1,0:T(2,128)(2,1)} %reshape.186, bf16[]{:T(256)} %constant.59), dimensions={1}, to_apply=%all_to_all.15.reduce_sub_computation | reduce | bytes 5242882 | tf_op jit(solution)/shard_map/all_to_all | solution.py:100
  417.6 5.2 %reshape.151 = bf16[640,2048]{1,0:T(8,128)(2,1)S(1)} reshape(bf16[64,20480]{1,0:T(8,128)(2,1)} %reduce.5) | data formatting | bytes 5242880 | tf_op jit(solution)/shard_map/reshape | solution.py:101
  426.1 5.6 %reshape.152 = f32[256,2,2048]{2,1,0:T(2,128)} reshape(bf16[512,2048]{1,0:T(8,128)(2,1)} %gather_fusion.1) | data formatting | bytes 6291456 | tf_op jit(solution)/shard_map/convert_element_type | solution.py:102
  431.8 9.0 %multiply_reduce_fusion = f32[256,2048]{1,0:T(8,128)S(1)} fusion(f32[256,2,2048]{2,1,0:T(2,128)} %reshape.152, f32[256,2]{1,0:T(8,128)S(1)} %copy.72), kind=kLoop, calls=%fused_computation.29 | loop fusion | flops 1572864 | bytes 6293504 | tf_op jit(solution)/shard_map/reduce_sum | solution.py:103
  (96 shorter events, 82.9 us)
Async XLA Ops:
  1.5 29.0 %copy-start.12 = (s32[1,256,2]{1,2,0:T(2,128)S(1)}, s32[1,256,2]{1,2,0:T(2,128)}, u32[]{:S(2)}) copy-start(s32[1,256,2]{1,2,0:T(2,128)} %param.14) | copy-start | bytes 6148
  1.5 26.5 %collective-permute-start = (bf16[1,256,2048]{1,2,0:T(8,128)(2,1)S(1)}, bf16[1,256,2048]{1,2,0:T(8,128)(2,1)S(1)}, u32[]{:S(2)}, u32[]{:S(2)}) collective-permute-start(bf16[1,256,2048]{1,2,0:T(8,128)(2,1)S(1)} %copy.59), channel_id=1, source_target_pairs={{0,128},{64,192},{128,0},{192,64},{1,129},{65,193},{129,1},{193,65... | collective-permute-start | bytes 3145736 | tf_op jit(solution)/shard_map/ppermute | solution.py:12
  28.0 1.0 copy-start.3
  30.5 34.8 %collective-permute-start.3 = (bf16[2,1,256,2048]{2,3,1,0:T(8,128)(2,1)}, bf16[2,1,256,2048]{2,3,1,0:T(8,128)(2,1)}, u32[]{:S(2)}, u32[]{:S(2)}) collective-permute-start(bf16[2,1,256,2048]{2,3,1,0:T(8,128)(2,1)} %pad_maximum_fusion.2), channel_id=1, source_target_pairs={{0,64},{64,0},{128,192},{192,128},{1,65},{65,1},{129,193},{193,129... | collective-permute-start | bytes 6291464 | tf_op jit(solution)/shard_map/ppermute | solution.py:16
  32.0 27.5 %collective-permute-start.1 = (bf16[1,256,2048]{2,1,0:T(8,128)(2,1)}, bf16[1,256,2048]{2,1,0:T(8,128)(2,1)}, u32[]{:S(2)}, u32[]{:S(2)}) collective-permute-start(bf16[1,256,2048]{2,1,0:T(8,128)(2,1)} %param.11), channel_id=1, source_target_pairs={{0,128},{64,192},{128,0},{192,64},{1,129},{65,193},{129,1},{193,65... | collective-permute-start | bytes 3145736 | tf_op jit(solution)/shard_map/ppermute | solution.py:12
  35.0 3.9 copy-start.2
  38.9 4.8 %copy-start.4 = (bf16[1,256,2048]{1,2,0:T(8,128)(2,1)S(1)}, bf16[1,256,2048]{1,2,0:T(8,128)(2,1)}, u32[]{:S(2)}) copy-start(bf16[1,256,2048]{1,2,0:T(8,128)(2,1)} %copy-done.3) | copy-start | bytes 3145732
  62.6 24.7 %collective-permute-start.2 = (bf16[2,1,256,2048]{3,2,1,0:T(8,128)(2,1)}, bf16[2,1,256,2048]{3,2,1,0:T(8,128)(2,1)}, u32[]{:S(2)}, u32[]{:S(2)}) collective-permute-start(bf16[2,1,256,2048]{3,2,1,0:T(8,128)(2,1)} %pad_maximum_fusion.1), channel_id=1, source_target_pairs={{0,64},{64,0},{128,192},{192,128},{1,65},{65,1},{129,193},{193,129... | collective-permute-start | bytes 6291464 | tf_op jit(solution)/shard_map/ppermute | solution.py:16
  62.6 50.1 %collective-permute-start.4 = (bf16[2048,512]{1,0:T(8,128)(2,1)}, bf16[2048,512]{1,0:T(8,128)(2,1)}, u32[]{:S(2)}, u32[]{:S(2)}) collective-permute-start(bf16[2048,512]{1,0:T(8,128)(2,1)} %bitcast.42), channel_id=1, source_target_pairs={{0,128},{64,192},{128,0},{192,64},{1,129},{65,193},{129,1},{193,65... | collective-permute-start | bytes 6291464 | tf_op jit(solution)/shard_map/ppermute | solution.py:12
  67.0 2.0 copy-start.8
  89.0 1.8 copy-start.7
  101.9 11.3 %copy-start.6 = (bf16[1,256,2048]{2,1,0:T(8,128)(2,1)S(1)}, bf16[1,256,2048]{2,1,0:T(8,128)(2,1)}, u32[]{:S(2)}) copy-start(bf16[1,256,2048]{2,1,0:T(8,128)(2,1)} %param.12) | copy-start | bytes 3145732
  103.9 10.6 %copy-start.11 = (f32[2048]{0:T(1024)S(1)}, f32[2048]{0:T(1024)}, u32[]{:S(2)}) copy-start(f32[2048]{0:T(1024)} %param.13) | copy-start | bytes 24580
  112.6 26.8 %collective-permute-start.5 = (bf16[256,2048]{1,0:T(8,128)(2,1)}, bf16[256,2048]{1,0:T(8,128)(2,1)}, u32[]{:S(2)}, u32[]{:S(2)}) collective-permute-start(bf16[256,2048]{1,0:T(8,128)(2,1)} %bitcast.114), channel_id=1, source_target_pairs={{0,128},{64,192},{128,0},{192,64},{1,129},{65,193},{129,1},{193,65... | collective-permute-start | bytes 3145736 | tf_op jit(solution)/shard_map/ppermute | solution.py:12
  113.5 1.0 copy-start
  175.0 74.1 %all-to-all-start = ((bf16[64,2,10240]{2,1,0:T(2,128)(2,1)}), bf16[64,2,10240]{2,1,0:T(2,128)(2,1)S(1)}, u32[]{:S(2)}, u32[]{:S(2)}) async-start(bf16[64,2,10240]{2,1,0:T(2,128)(2,1)} %reshape.183), calls=%async_computation | async-start | bytes 5242880 | tf_op jit(solution)/shard_map/all_to_all | solution.py:88
  192.2 4.7 %copy-start.9 = (bf16[1,256,2048]{2,1,0:T(8,128)(2,1)S(1)}, bf16[1,256,2048]{2,1,0:T(8,128)(2,1)}, u32[]{:S(2)}) copy-start(bf16[1,256,2048]{2,1,0:T(8,128)(2,1)} %param.17) | copy-start | bytes 3145732
  196.9 90.1 %collective-permute-start.6 = (bf16[2,2048,512]{2,1,0:T(8,128)(2,1)}, bf16[2,2048,512]{2,1,0:T(8,128)(2,1)}, u32[]{:S(2)}, u32[]{:S(2)}) collective-permute-start(bf16[2,2048,512]{2,1,0:T(8,128)(2,1)} %pad_maximum_fusion), channel_id=1, source_target_pairs={{0,64},{64,0},{128,192},{192,128},{1,65},{65,1},{129,193},{193,129... | collective-permute-start | bytes 12582920 | tf_op jit(solution)/shard_map/ppermute | solution.py:16
  199.6 93.6 %collective-permute-start.7 = (bf16[2,256,2048]{2,1,0:T(8,128)(2,1)}, bf16[2,256,2048]{2,1,0:T(8,128)(2,1)}, u32[]{:S(2)}, u32[]{:S(2)}) collective-permute-start(bf16[2,256,2048]{2,1,0:T(8,128)(2,1)} %pad_maximum_fusion.3), channel_id=1, source_target_pairs={{0,64},{64,0},{128,192},{192,128},{1,65},{65,1},{129,193},{193,129... | collective-permute-start | bytes 6291464 | tf_op jit(solution)/shard_map/ppermute | solution.py:16
  280.6 2.3 copy-start.5
  282.9 3.2 copy-start.10
  325.7 6.3 %copy-start.13 = (f32[1,256,2]{1,2,0:T(2,128)S(1)}, f32[1,256,2]{1,2,0:T(2,128)}, u32[]{:S(2)}) copy-start(f32[1,256,2]{1,2,0:T(2,128)} %param.15) | copy-start | bytes 6148
  325.7 67.7 %all-to-all-start.1 = ((bf16[64,2,10240]{2,1,0:T(2,128)(2,1)}), bf16[64,2,10240]{2,1,0:T(2,128)(2,1)S(1)}, u32[]{:S(2)}, u32[]{:S(2)}) async-start(bf16[64,2,10240]{2,1,0:T(2,128)(2,1)} %reshape.185), calls=%async_computation.1 | async-start | bytes 5242880 | tf_op jit(solution)/shard_map/all_to_all | solution.py:100
  431.8 9.0 %copy-start.1 = (bf16[1,256,2048]{2,1,0:T(8,128)(2,1)S(1)}, bf16[1,256,2048]{2,1,0:T(8,128)(2,1)}, u32[]{:S(2)}) copy-start(bf16[1,256,2048]{2,1,0:T(8,128)(2,1)} %copy-done) | copy-start | bytes 3145732

commit v3 on v2

--- a/solution.py
+++ b/solution.py
@@ -80,9 +80,9 @@
         .at[destination]
         .set(jnp.arange(token_count * top_count, dtype=jnp.int32) // top_count)
     )
-    normed, gate_up_far, down_far = lax.optimization_barrier((normed, gate_up_far, down_far))
+    normed, gate_up_far = lax.optimization_barrier((normed, gate_up_far))
     send_buffer = normed.reshape(token_count, feature_count)[slot_token]
-    send_buffer = send_buffer.reshape(expert_count, capacity * feature_count)
+    send_buffer = send_buffer.reshape(expert_count, capacity * 8, feature_count // 8)
     gate_up_blocks = near_blocks(gate_up_local, gate_up_far)
     down_blocks = near_blocks(down_local, down_far)
     portion = lax.all_to_all(send_buffer, "exp", split_axis=0, concat_axis=0, tiled=True)

time: 449 us -> 322 us (0.72)
  other arithmetic: 97.6 us -> 31.7 us
  local copies, waits for them, and re-layouts: 96.3 us -> 61.2 us
  waiting for transfers between devices: 182 us -> 158 us
    all_to_all x4 -> x0, other arithmetic: 64.8 us -> none  [the longest x2 33.2 us: shards(): lax.all_to_all(summed, 'exp', split_axis=0, concat_axis=0, tiled=True)]
    all_to_all x1, waiting for transfers between devices: 48.6 us -> 6.36 us  [shards(): lax.all_to_all(send_buffer, 'exp', split_axis=0, concat_axis=0, tiled=True)]
    all_to_all x3 -> x0, local copies, waits for them, and re-layouts: 20.4 us -> none  [the longest x2 12.3 us: shards(): lax.all_to_all(send_buffer, 'exp', split_axis=0, concat_axis=0, tiled=True)]
    unnamed x37, local copies, waits for them, and re-layouts: 30.9 us -> 11 us
    ppermute x4, waiting for transfers between devices: 72 us -> 90.5 us  [far_block(): return lax.ppermute(block, 'ctx', perm=[(c, c ^ 2) for c in range(4)])]
    reshape x0 -> x2, local copies, waits for them, and re-layouts: none -> 8.45 us  [the longest x1 5.29 us: shards(): send_buffer.reshape(expert_count, capacity * 8, feature_count // 8)]
  transfers between devices with their start and end apart: 10 -> 10, of which waited for: 6 -> 6; matrix products, arithmetic and copies ran while one was open for 26% -> 28% of each run, Pallas kernels for 0% -> 0%
where the time goes in v3:
time: 322 us; the launch traced here: 316 us
  waiting for transfers between devices  158 us (49%)
  local copies, waits for them, and re-layouts  61.2 us (19%)
  matrix products  40.8 us (13%)
  other arithmetic  31.7 us (10%)
  starting transfers between devices  23.1 us (7%)
    ppermute x4, waiting for transfers between devices, far_block(): return lax.ppermute(block, 'ctx', perm=[(c, c ^ 2) for c in range(4)])  90.5 us
    all_to_all x1, waiting for transfers between devices, shards(): lax.all_to_all(summed, 'exp', split_axis=0, concat_axis=0, tiled=True)  61.6 us
    dot_general x4, matrix products, shards(): jnp.dot(flattened, gate_up_block, preferred_element_type=jnp.float32)  13.4 us
    all_to_all x1, starting transfers between devices, shards(): lax.all_to_all(send_buffer, 'exp', split_axis=0, concat_axis=0, tiled=True)  13 us
    unnamed x37, local copies, waits for them, and re-layouts  11 us
    dot_general x1, matrix products, shards(): jnp.einsum('cqhk,ckhd->cqhd', expo.astype(jnp.bfloat16), value_heads, pre...  11 us
    another operation x4, other arithmetic, near_blocks(): jnp.stack([block, far])  10.9 us
    dot_general x1, matrix products, shards(): jnp.einsum('cqhd,ckhd->cqhk', query_heads, key_heads, preferred_element_t...  9.75 us
  transfers between devices with their start and end apart: 10, of which 6 were waited for; matrix products, arithmetic and copies ran while one was open for 28% of the time, Pallas kernels for 0%

profile of v3, /device:TPU:4, one launch (start us, length us, event | category | flops | bytes accessed | tf_op | source)
XLA Modules:
  0.0 316.1 jit_solution(4225791185875755024)
XLA Ops:
  3.8 24.2 %collective-permute-done = bf16[1,256,2048]{1,2,0:T(8,128)(2,1)S(1)} collective-permute-done((bf16[1,256,2048]{1,2,0:T(8,128)(2,1)S(1)}, bf16[1,256,2048]{1,2,0:T(8,128)(2,1)S(1)}, u32[]{:S(2)}, u32[]{:S(2)}) %collective-permute-start) | collective-permute-done | bytes 1048608 | tf_op jit(solution)/shard_map/ppermute | solution.py:12
  44.9 14.6 %collective-permute-done.1 = bf16[1,256,2048]{2,1,0:T(8,128)(2,1)} collective-permute-done((bf16[1,256,2048]{2,1,0:T(8,128)(2,1)}, bf16[1,256,2048]{2,1,0:T(8,128)(2,1)}, u32[]{:S(2)}, u32[]{:S(2)}) %collective-permute-start.1) | collective-permute-done | bytes 1048608 | tf_op jit(solution)/shard_map/ppermute | solution.py:12
  69.0 9.7 %bitcast_reduce_fusion = (f32[256,16]{0,1:T(8,128)S(1)}, f32[16,1024,256]{2,1,0:T(8,128)}) fusion(bf16[256,16,128]{2,1,0:T(8,128)(2,1)} %bitcast.110, bf16[1,256,16,128]{3,1,2,0:T(8,128)(2,1)S(1)} %copy.28, bf16[1,256,16,128]{3,1,2,0:T(8,128)(2,1)} %copy.27, bf16[1,256,16,128]{3,1,2,0:T(8,128)(2,1)} %copy.26, bf16[1,256,16,128]{3,1,2,0:T(8,128)(2,1)S(1)} %copy-done.8), kind=kOutput, calls=%fused_computation.4 | convolution fusion | flops 1098903552 | bytes 22036480 | tf_op jit(solution)/shard_map/cqhd,ckhd->cqhk/dot_general | solution.py:49
  78.7 8.5 %fusion.1 = f32[256,16]{0,1:T(8,128)S(1)} fusion(f32[16,1024,256]{2,1,0:T(8,128)} %get-tuple-element.22, f32[256,16]{0,1:T(8,128)S(1)} %broadcast_maximum_fusion), kind=kLoop, calls=%fused_computation.6 | loop fusion | flops 12578816 | bytes 16809984 | tf_op jit(solution)/shard_map/reduce_sum | solution.py:54
  90.8 11.0 %bitcast_divide_fusion = f32[1,256,16,128]{1,3,2,0:T(8,128)} fusion(f32[256,16]{0,1:T(8,128)S(1)} %fusion.1, f32[16,1024,256]{2,1,0:T(8,128)} %get-tuple-element.22, f32[256,16]{0,1:T(8,128)S(1)} %broadcast_maximum_fusion, bf16[1,256,16,128]{1,3,2,0:T(8,128)(2,1)S(1)} %bitcast.113, bf16[1,256,16,128]{1,3,2,0:T(8,128)(2,1)} %bitcast.112, ...), kind=kOutput, calls=%fused_computation.48 | convolution fusion | flops 1103626240 | bytes 23101440 | tf_op jit(solution)/shard_map/cqhk,ckhd->cqhd/dot_general | solution.py:55
  105.5 7.1 %collective-permute-done.4 = bf16[2048,512]{1,0:T(8,128)(2,1)} collective-permute-done((bf16[2048,512]{1,0:T(8,128)(2,1)}, bf16[2048,512]{1,0:T(8,128)(2,1)}, u32[]{:S(2)}, u32[]{:S(2)}) %collective-permute-start.4) | collective-permute-done | bytes 2097184 | tf_op jit(solution)/shard_map/ppermute | solution.py:12
  112.6 4.1 %gather_fusion = bf16[640,2048]{1,0:T(8,128)(2,1)} fusion(bf16[256,2048]{1,0:T(8,128)(2,1)S(1)} %bitcast.99, s32[1024]{0:T(1024)S(1)} %pad_clamp_fusion.1), kind=kCustom, calls=%fused_computation | custom fusion | bytes 5245440 | tf_op jit(solution)/shard_map/gather | solution.py:84
  116.7 5.3 %reshape.146 = bf16[64,80,256]{2,1,0:T(8,128)(2,1)} reshape(bf16[640,2048]{1,0:T(8,128)(2,1)} %gather_fusion) | data formatting | bytes 5242880 | tf_op jit(solution)/shard_map/reshape | solution.py:85
  122.0 13.0 %all-to-all-start = ((bf16[64,80,256]{2,1,0:T(8,128)(2,1)}), bf16[64,80,256]{2,1,0:T(8,128)(2,1)S(1)}, u32[]{:S(2)}, u32[]{:S(2)}) async-start(bf16[64,80,256]{2,1,0:T(8,128)(2,1)} %reshape.146), calls=%async_computation | async-start | bytes 5242880 | tf_op jit(solution)/shard_map/all_to_all | solution.py:88
  134.9 4.4 %stack_reshape_squeeze.3 = bf16[1,2048,512]{2,1,0:T(8,128)(2,1)} reshape(bf16[1,2048,2,256]{3,2,1,0:T(2,128)(2,1)} %param.16) | data formatting | bytes 4194304 | tf_op jit(solution)/shard_map/stack;reshape;squeeze | solution.py:16
  139.3 4.6 %pad_maximum_fusion = bf16[2,2048,512]{2,1,0:T(8,128)(2,1)} fusion(bf16[1,2048,512]{2,1,0:T(8,128)(2,1)} %bitcast.27, bf16[1,2048,512]{2,1,0:T(8,128)(2,1)} %stack_reshape_squeeze.3), kind=kLoop, calls=%fused_computation.28 | loop fusion | flops 2097152 | bytes 8388608 | tf_op jit(solution)/shard_map/stack | solution.py:16
  144.7 44.7 %collective-permute-done.5 = bf16[256,2048]{1,0:T(8,128)(2,1)S(1)} collective-permute-done((bf16[256,2048]{1,0:T(8,128)(2,1)S(1)}, bf16[256,2048]{1,0:T(8,128)(2,1)S(1)}, u32[]{:S(2)}, u32[]{:S(2)}) %collective-permute-start.5) | collective-permute-done | bytes 1048608 | tf_op jit(solution)/shard_map/ppermute | solution.py:12
  191.1 6.4 %all-to-all-done = bf16[64,80,256]{2,1,0:T(8,128)(2,1)S(1)} async-done(((bf16[64,80,256]{2,1,0:T(8,128)(2,1)}), bf16[64,80,256]{2,1,0:T(8,128)(2,1)S(1)}, u32[]{:S(2)}, u32[]{:S(2)}) %all-to-all-start) | async-done | bytes 2621472 | tf_op jit(solution)/shard_map/all_to_all | solution.py:88
  197.4 3.2 %reshape.147 = bf16[640,2048]{1,0:T(8,128)(2,1)} reshape(bf16[64,80,256]{2,1,0:T(8,128)(2,1)S(1)} %all-to-all-done) | data formatting | bytes 5242880 | tf_op jit(solution)/shard_map/reshape | solution.py:89
  200.6 4.0 %fusion.60 = f32[640,512]{1,0:T(8,128)S(1)} fusion(bf16[640,2048]{1,0:T(8,128)(2,1)} %reshape.147, bf16[2048,512]{1,0:T(8,128)(2,1)} %bitcast.42), kind=kOutput, calls=%fused_computation.100 | convolution fusion | flops 1342177280 | bytes 6029312 | tf_op jit(solution)/shard_map/dot_general | solution.py:92
  206.4 3.2 %fusion.61 = f32[640,512]{1,0:T(8,128)S(1)} fusion(bf16[640,2048]{1,0:T(8,128)(2,1)S(1)} %copy-done.5, bf16[2048,512]{1,0:T(8,128)(2,1)} %collective-permute-done.4), kind=kOutput, calls=%fused_computation.101 | convolution fusion | flops 1342177280 | bytes 6029312 | tf_op jit(solution)/shard_map/dot_general | solution.py:92
  210.5 3.1 fusion.25
  221.6 3.2 reshape.148
  224.7 6.3 %all-to-all-start.1 = ((bf16[64,80,256]{2,1,0:T(8,128)(2,1)}), bf16[64,80,256]{2,1,0:T(8,128)(2,1)}, u32[]{:S(2)}, u32[]{:S(2)}) async-start(bf16[64,80,256]{2,1,0:T(8,128)(2,1)} %reshape.148), calls=%async_computation.1 | async-start | bytes 5242880 | tf_op jit(solution)/shard_map/all_to_all | solution.py:100
  231.2 61.6 %all-to-all-done.1 = bf16[64,80,256]{2,1,0:T(8,128)(2,1)} async-done(((bf16[64,80,256]{2,1,0:T(8,128)(2,1)}), bf16[64,80,256]{2,1,0:T(8,128)(2,1)}, u32[]{:S(2)}, u32[]{:S(2)}) %all-to-all-start.1) | async-done | bytes 2621472 | tf_op jit(solution)/shard_map/all_to_all | solution.py:100
  292.7 3.9 %reshape.149 = bf16[640,2048]{1,0:T(8,128)(2,1)S(1)} reshape(bf16[64,80,256]{2,1,0:T(8,128)(2,1)} %all-to-all-done.1) | data formatting | bytes 5242880 | tf_op jit(solution)/shard_map/reshape | solution.py:101
  296.6 3.3 %gather_fusion.1 = bf16[512,2048]{1,0:T(8,128)(2,1)} fusion(bf16[640,2048]{1,0:T(8,128)(2,1)S(1)} %reshape.149, s32[1024]{0:T(1024)S(1)} %pad_clamp_fusion), kind=kCustom, calls=%fused_computation.1 | custom fusion | bytes 4196352 | tf_op jit(solution)/shard_map/gather | solution.py:101
  299.9 5.4 %reshape.150 = f32[256,2,2048]{2,1,0:T(2,128)} reshape(bf16[512,2048]{1,0:T(8,128)(2,1)} %gather_fusion.1) | data formatting | bytes 6291456 | tf_op jit(solution)/shard_map/convert_element_type | solution.py:102
  305.4 9.0 %multiply_reduce_fusion = f32[256,2048]{1,0:T(8,128)S(1)} fusion(f32[256,2,2048]{2,1,0:T(2,128)} %reshape.150, f32[256,2]{1,0:T(8,128)S(1)} %copy.32), kind=kLoop, calls=%fused_computation.29 | loop fusion | flops 1572864 | bytes 6293504 | tf_op jit(solution)/shard_map/reduce_sum | solution.py:103
  (91 shorter events, 51.7 us)
Async XLA Ops:
  1.5 29.1 %copy-start.14 = (s32[1,256,2]{1,2,0:T(2,128)S(1)}, s32[1,256,2]{1,2,0:T(2,128)}, u32[]{:S(2)}) copy-start(s32[1,256,2]{1,2,0:T(2,128)} %param.14) | copy-start | bytes 6148
  1.5 26.5 %collective-permute-start = (bf16[1,256,2048]{1,2,0:T(8,128)(2,1)S(1)}, bf16[1,256,2048]{1,2,0:T(8,128)(2,1)S(1)}, u32[]{:S(2)}, u32[]{:S(2)}) collective-permute-start(bf16[1,256,2048]{1,2,0:T(8,128)(2,1)S(1)} %copy.19), channel_id=1, source_target_pairs={{0,128},{64,192},{128,0},{192,64},{1,129},{65,193},{129,1},{193,65... | collective-permute-start | bytes 3145736 | tf_op jit(solution)/shard_map/ppermute | solution.py:12
  30.5 34.8 %collective-permute-start.3 = (bf16[2,1,256,2048]{2,3,1,0:T(8,128)(2,1)}, bf16[2,1,256,2048]{2,3,1,0:T(8,128)(2,1)}, u32[]{:S(2)}, u32[]{:S(2)}) collective-permute-start(bf16[2,1,256,2048]{2,3,1,0:T(8,128)(2,1)} %pad_maximum_fusion.2), channel_id=1, source_target_pairs={{0,64},{64,0},{128,192},{192,128},{1,65},{65,1},{129,193},{193,129... | collective-permute-start | bytes 6291464 | tf_op jit(solution)/shard_map/ppermute | solution.py:16
  32.1 27.5 %collective-permute-start.1 = (bf16[1,256,2048]{2,1,0:T(8,128)(2,1)}, bf16[1,256,2048]{2,1,0:T(8,128)(2,1)}, u32[]{:S(2)}, u32[]{:S(2)}) collective-permute-start(bf16[1,256,2048]{2,1,0:T(8,128)(2,1)} %param.11), channel_id=1, source_target_pairs={{0,128},{64,192},{128,0},{192,64},{1,129},{65,193},{129,1},{193,65... | collective-permute-start | bytes 3145736 | tf_op jit(solution)/shard_map/ppermute | solution.py:12
  35.0 3.9 %copy-start.2 = (bf16[1,2048,2,256]{3,2,1,0:T(2,128)(2,1)S(1)}, bf16[1,2048,2,256]{3,2,1,0:T(2,128)(2,1)}, u32[]{:S(2)}) copy-start(bf16[1,2048,2,256]{3,2,1,0:T(2,128)(2,1)} %param.16) | copy-start | bytes 6291460
  38.9 4.8 %copy-start.4 = (bf16[1,256,2048]{1,2,0:T(8,128)(2,1)S(1)}, bf16[1,256,2048]{1,2,0:T(8,128)(2,1)}, u32[]{:S(2)}) copy-start(bf16[1,256,2048]{1,2,0:T(8,128)(2,1)} %copy-done.3) | copy-start | bytes 3145732
  62.6 24.6 %collective-permute-start.2 = (bf16[2,1,256,2048]{3,2,1,0:T(8,128)(2,1)}, bf16[2,1,256,2048]{3,2,1,0:T(8,128)(2,1)}, u32[]{:S(2)}, u32[]{:S(2)}) collective-permute-start(bf16[2,1,256,2048]{3,2,1,0:T(8,128)(2,1)} %pad_maximum_fusion.1), channel_id=1, source_target_pairs={{0,64},{64,0},{128,192},{192,128},{1,65},{65,1},{129,193},{193,129... | collective-permute-start | bytes 6291464 | tf_op jit(solution)/shard_map/ppermute | solution.py:16
  62.6 50.0 %collective-permute-start.4 = (bf16[2048,512]{1,0:T(8,128)(2,1)}, bf16[2048,512]{1,0:T(8,128)(2,1)}, u32[]{:S(2)}, u32[]{:S(2)}) collective-permute-start(bf16[2048,512]{1,0:T(8,128)(2,1)} %bitcast.42), channel_id=1, source_target_pairs={{0,128},{64,192},{128,0},{192,64},{1,129},{65,193},{129,1},{193,65... | collective-permute-start | bytes 6291464 | tf_op jit(solution)/shard_map/ppermute | solution.py:12
  67.0 2.0 copy-start.8
  88.9 1.8 copy-start.7
  101.8 2.0 copy-start.6
  103.8 1.4 copy-start.13
  122.0 75.5 %all-to-all-start = ((bf16[64,80,256]{2,1,0:T(8,128)(2,1)}), bf16[64,80,256]{2,1,0:T(8,128)(2,1)S(1)}, u32[]{:S(2)}, u32[]{:S(2)}) async-start(bf16[64,80,256]{2,1,0:T(8,128)(2,1)} %reshape.146), calls=%async_computation | async-start | bytes 5242880 | tf_op jit(solution)/shard_map/all_to_all | solution.py:88
  139.3 4.6 %copy-start.9 = (bf16[1,256,2048]{2,1,0:T(8,128)(2,1)S(1)}, bf16[1,256,2048]{2,1,0:T(8,128)(2,1)}, u32[]{:S(2)}) copy-start(bf16[1,256,2048]{2,1,0:T(8,128)(2,1)} %param.17) | copy-start | bytes 3145732
  143.9 66.5 %collective-permute-start.6 = (bf16[2,2048,512]{2,1,0:T(8,128)(2,1)}, bf16[2,2048,512]{2,1,0:T(8,128)(2,1)}, u32[]{:S(2)}, u32[]{:S(2)}) collective-permute-start(bf16[2,2048,512]{2,1,0:T(8,128)(2,1)} %pad_maximum_fusion), channel_id=1, source_target_pairs={{0,64},{64,0},{128,192},{192,128},{1,65},{65,1},{129,193},{193,129... | collective-permute-start | bytes 12582920 | tf_op jit(solution)/shard_map/ppermute | solution.py:16
  143.9 45.5 %collective-permute-start.5 = (bf16[256,2048]{1,0:T(8,128)(2,1)S(1)}, bf16[256,2048]{1,0:T(8,128)(2,1)S(1)}, u32[]{:S(2)}, u32[]{:S(2)}) collective-permute-start(bf16[256,2048]{1,0:T(8,128)(2,1)S(1)} %bitcast.114), channel_id=1, source_target_pairs={{0,128},{64,192},{128,0},{192,64},{1,129},{65,193},{129,1},{193,65... | collective-permute-start | bytes 3145736 | tf_op jit(solution)/shard_map/ppermute | solution.py:12
  189.4 1.7 copy-start.11
  191.1 25.6 %collective-permute-start.7 = (bf16[2,256,2048]{2,1,0:T(8,128)(2,1)}, bf16[2,256,2048]{2,1,0:T(8,128)(2,1)}, u32[]{:S(2)}, u32[]{:S(2)}) collective-permute-start(bf16[2,256,2048]{2,1,0:T(8,128)(2,1)} %pad_maximum_fusion.3), channel_id=1, source_target_pairs={{0,64},{64,0},{128,192},{192,128},{1,65},{65,1},{129,193},{193,129... | collective-permute-start | bytes 6291464 | tf_op jit(solution)/shard_map/ppermute | solution.py:16
  200.6 4.0 %copy-start.10 = (bf16[1,256,2048]{2,1,0:T(8,128)(2,1)S(1)}, bf16[1,256,2048]{2,1,0:T(8,128)(2,1)}, u32[]{:S(2)}) copy-start(bf16[1,256,2048]{2,1,0:T(8,128)(2,1)} %param.17) | copy-start | bytes 3145732
  204.6 1.7 copy-start.5
  206.4 3.2 %copy-start.12 = (bf16[256,2048]{1,0:T(8,128)(2,1)S(1)}, bf16[256,2048]{1,0:T(8,128)(2,1)}, u32[]{:S(2)}) copy-start(bf16[256,2048]{1,0:T(8,128)(2,1)} %copy-done.11) | copy-start | bytes 3145732
  224.7 6.3 %copy-start.15 = (f32[1,256,2]{1,2,0:T(2,128)S(1)}, f32[1,256,2]{1,2,0:T(2,128)}, u32[]{:S(2)}) copy-start(f32[1,256,2]{1,2,0:T(2,128)} %param.15) | copy-start | bytes 6148
  224.7 68.0 %all-to-all-start.1 = ((bf16[64,80,256]{2,1,0:T(8,128)(2,1)}), bf16[64,80,256]{2,1,0:T(8,128)(2,1)}, u32[]{:S(2)}, u32[]{:S(2)}) async-start(bf16[64,80,256]{2,1,0:T(8,128)(2,1)} %reshape.148), calls=%async_computation.1 | async-start | bytes 5242880 | tf_op jit(solution)/shard_map/all_to_all | solution.py:100
  305.4 9.0 %copy-start.1 = (bf16[1,256,2048]{2,1,0:T(8,128)(2,1)S(1)}, bf16[1,256,2048]{2,1,0:T(8,128)(2,1)}, u32[]{:S(2)}) copy-start(bf16[1,256,2048]{2,1,0:T(8,128)(2,1)} %copy-done) | copy-start | bytes 3145732
  (2 other events, 2.0 us)
